TPU v7x, 512 devices: a whole 4x8x8 slice. The times are simulated.
512 devices in a mesh: tm: 64 (over y, x, core), head: 8 (over z).
Axes of the slice: x: 4, y: 8, z: 8, core: 2. Of those that a mesh axis runs over, the one named last changes fastest.
Arguments:
- queries: bfloat16 [24576, 5120], P('tm', 'head')
- keys: bfloat16 [24576, 5120], P('tm', 'head')
- values: bfloat16 [24576, 5120], P('tm', 'head')
- text_keys: bfloat16 [512, 5120], P('tm', 'head'), may hold values from -6 to 6
- text_values: bfloat16 [512, 5120], P('tm', 'head')
- out_weight: bfloat16 [5120, 5120], P('head', 'tm'), may hold values from -0.25 to 0.25
- windows: int32 [64], replicated, may hold values from 0 to 4, as said below
- lengths: int32 [64], replicated, may hold values from 96 to 384, as said below
Outputs:
- mixed: bfloat16 [24576, 5120], P('tm', 'head')
Inputs may be any that keep to these rules, and one draw needn't show every extreme that they name: windows reach 4 for some frame in every draw. `lengths`: some frame is full in every draw.
All inputs are finite; a program needn't handle non-finite values.
Results may differ from a plain program's by a relative error of at most 0.014.
Values may be sent and summed in bfloat16 or wider, within the bound.
No kernel may reach another device: no remote copies, remote signals or barrier semaphores. Data moves between devices by JAX's collectives and lax.ppermute only.
A program may use at most 64 MiB of HBM per device.

v0:
```python
import math
import jax
import jax.numpy as jnp
from jax import lax
from jax.sharding import PartitionSpec as P

HD = 128
WIN = 4


def from_behind(value, axis, steps):
    count = lax.axis_size(axis)
    initial, last = (max(0, -steps), min(count, count - steps))
    return lax.ppermute(value, axis, [(source, source + steps) for source in range(initial, last)])


def on_device(queries, keys, values, text_keys, text_values, out_weight, windows, lengths):
    rows = queries.shape[0]
    width = queries.shape[1]
    local_heads = width // HD
    scale = 1.0 / math.sqrt(HD)
    position = lax.axis_index("tm")
    text_k, text_v = (
        lax.all_gather(text_keys, "tm", axis=0, tiled=True),
        lax.all_gather(text_values, "tm", axis=0, tiled=True),
    )
    key_list = [keys]
    value_list = [values]
    for step in range(1, WIN + 1):
        moved_k, moved_v = from_behind((keys, values), "tm", step)
        key_list.append(moved_k)
        value_list.append(moved_v)
    token_ids = jnp.arange(rows, dtype=jnp.int32)
    own_window = windows[position]
    mask_list = []
    for step in range(WIN + 1):
        source = position - step
        usable = (step <= own_window) & (source >= 0)
        source_len = lengths[jnp.maximum(source, 0)]
        mask_list.append(usable & (token_ids < source_len))
    mask_list.append(jnp.ones((text_k.shape[0],), bool))
    key_mask = jnp.concatenate(mask_list)
    all_keys = jnp.concatenate(key_list + [text_k], axis=0)
    all_values = jnp.concatenate(value_list + [text_v], axis=0)
    head_outputs = []
    for head_index in range(local_heads):
        lower = head_index * HD
        query_h = queries[:, lower : lower + HD]
        key_h = all_keys[:, lower : lower + HD]
        value_h = all_values[:, lower : lower + HD]
        scores = (
            lax.dot_general(
                query_h, key_h, (((1,), (1,)), ((), ())), preferred_element_type=jnp.float32
            )
            * scale
        )
        scores = jnp.where(key_mask[None, :], scores, -jnp.inf)
        top = jnp.max(scores, axis=-1, keepdims=True)
        weights = jnp.exp(scores - top)
        total = jnp.sum(weights, axis=-1, keepdims=True)
        attended = (
            jnp.dot(weights.astype(jnp.bfloat16), value_h, preferred_element_type=jnp.float32)
            / total
        )
        head_outputs.append(attended.astype(jnp.bfloat16))
    attended_all = jnp.concatenate(head_outputs, axis=1)
    partial_out = jnp.dot(
        attended_all,
        lax.all_gather(out_weight, "tm", axis=1, tiled=True),
        preferred_element_type=jnp.float32,
    )
    return lax.psum_scatter(
        partial_out.astype(jnp.bfloat16), "head", scatter_dimension=1, tiled=True
    )


def solution(mesh):
    return jax.shard_map(
        on_device,
        mesh=mesh,
        in_specs=(
            P("tm", "head"),
            P("tm", "head"),
            P("tm", "head"),
            P("tm", "head"),
            P("tm", "head"),
            P("head", "tm"),
            P(),
            P(),
        ),
        out_specs=P("tm", "head"),
        check_vma=False,
    )
```

profile of v0, /device:TPU:1, one launch (start us, length us, event | category | flops | bytes accessed | tf_op | source)
XLA Modules:
  0.0 300.5 jit_solution(977108429921644657)
XLA Ops:
  6.5 0.7 all-gather.2.cloned.1.call-update
  7.3 0.0 reduce-scatter.4.cloned.1.call-start
  7.3 4.5 %collective-permute-start = (bf16[384,640]{1,0:T(8,128)(2,1)}, bf16[384,640]{1,0:T(8,128)(2,1)S(1)}, u32[]{:S(2)}, u32[]{:S(2)}) collective-permute-start(bf16[384,640]{1,0:T(8,128)(2,1)} %param.9), channel_id=1, source_target_pairs={{0,8},{8,16},{16,24},{24,32},{32,40},{40,48},{48,56},{56,64},{64,7... | collective-permute-start | bytes 1474568 | tf_op jit(solution)/shard_map/ppermute | solution.py:14
  11.8 3.1 %collective-permute-start.1 = (bf16[384,640]{1,0:T(8,128)(2,1)}, bf16[384,640]{1,0:T(8,128)(2,1)S(1)}, u32[]{:S(2)}, u32[]{:S(2)}) collective-permute-start(bf16[384,640]{1,0:T(8,128)(2,1)} %param.9), channel_id=1, source_target_pairs={{0,16},{8,24},{16,32},{24,40},{32,48},{40,56},{48,64},{56,72},{64,... | collective-permute-start | bytes 1474568 | tf_op jit(solution)/shard_map/ppermute | solution.py:14
  15.0 3.4 %collective-permute-start.2 = (bf16[384,640]{1,0:T(8,128)(2,1)}, bf16[384,640]{1,0:T(8,128)(2,1)S(1)}, u32[]{:S(2)}, u32[]{:S(2)}) collective-permute-start(bf16[384,640]{1,0:T(8,128)(2,1)} %param.9), channel_id=1, source_target_pairs={{0,24},{8,32},{16,40},{24,48},{32,56},{40,64},{48,72},{56,80},{64,... | collective-permute-start | bytes 1474568 | tf_op jit(solution)/shard_map/ppermute | solution.py:14
  18.4 3.4 %collective-permute-start.3 = (bf16[384,640]{1,0:T(8,128)(2,1)}, bf16[384,640]{1,0:T(8,128)(2,1)S(1)}, u32[]{:S(2)}, u32[]{:S(2)}) collective-permute-start(bf16[384,640]{1,0:T(8,128)(2,1)} %param.9), channel_id=1, source_target_pairs={{0,32},{8,40},{16,48},{24,56},{32,64},{40,72},{48,80},{56,88},{64,... | collective-permute-start | bytes 1474568 | tf_op jit(solution)/shard_map/ppermute | solution.py:14
  21.9 3.7 %collective-permute-start.4 = (bf16[384,640]{1,0:T(8,128)(2,1)}, bf16[384,640]{1,0:T(8,128)(2,1)S(1)}, u32[]{:S(2)}, u32[]{:S(2)}) collective-permute-start(bf16[384,640]{1,0:T(8,128)(2,1)} %param.10), channel_id=1, source_target_pairs={{0,8},{8,16},{16,24},{24,32},{32,40},{40,48},{48,56},{56,64},{64,7... | collective-permute-start | bytes 1474568 | tf_op jit(solution)/shard_map/ppermute | solution.py:14
  25.6 1.2 dynamic_slice.18
  30.1 1.5 fusion.95
  31.6 0.6 fusion.90
  32.2 0.3 dynamic-update-slice.17
  32.4 0.6 fusion.91
  33.1 0.3 dynamic-update-slice.18
  33.3 0.6 fusion.92
  34.0 0.3 dynamic-update-slice.19
  34.2 0.6 fusion.93
  34.9 0.3 dynamic-update-slice.20
  35.1 0.7 fusion.94
  35.8 0.3 dynamic-update-slice.21
  36.0 0.2 dynamic-update-slice.22
  36.3 74.3 %all_gather.9 = bf16[512,640]{1,0:T(8,128)(2,1)S(1)} all-gather(bf16[8,640]{1,0:T(8,128)(2,1)} %param.11), channel_id=1, replica_groups=mesh['tm'=64,'head'=8] {'tm'}, dimensions={0}, use_global_device_ids=true | all-gather | bytes 665600 | tf_op jit(solution)/shard_map/all_gather | solution.py:24
  110.6 48.6 %all_gather.10 = bf16[512,640]{1,0:T(8,128)(2,1)S(1)} all-gather(bf16[8,640]{1,0:T(8,128)(2,1)} %param.12), channel_id=1, replica_groups=mesh['tm'=64,'head'=8] {'tm'}, dimensions={0}, use_global_device_ids=true | all-gather | bytes 665600 | tf_op jit(solution)/shard_map/all_gather | solution.py:25
  159.3 1.1 constant_dynamic-update-slice_fusion.5
  160.3 1.1 constant_dynamic-update-slice_fusion.11
  161.4 2.3 collective-permute-start.5
  163.7 0.1 constant_dynamic-update-slice_fusion.4
  163.8 0.0 collective-permute-done.1
  163.8 4.6 %collective-permute-start.6 = (bf16[384,640]{1,0:T(8,128)(2,1)S(1)}, bf16[384,640]{1,0:T(8,128)(2,1)S(1)}, u32[]{:S(2)}, u32[]{:S(2)}) collective-permute-start(bf16[384,640]{1,0:T(8,128)(2,1)S(1)} %copy-done), channel_id=1, source_target_pairs={{0,24},{8,32},{16,40},{24,48},{32,56},{40,64},{48,72},{56,80},{64,... | collective-permute-start | bytes 1474568 | tf_op jit(solution)/shard_map/ppermute | solution.py:14
  168.5 0.1 constant_dynamic-update-slice_fusion.3
  168.6 0.0 collective-permute-done.2
  168.6 2.3 collective-permute-start.7
  170.9 0.1 constant_dynamic-update-slice_fusion.2
  170.9 0.0 copy-start.1
  170.9 0.1 constant_dynamic-update-slice_fusion.1
  171.0 0.1 constant_dynamic-update-slice_fusion.10
  171.1 3.4 %collective-permute-done.5 = bf16[384,640]{1,0:T(8,128)(2,1)S(1)} collective-permute-done((bf16[384,640]{1,0:T(8,128)(2,1)}, bf16[384,640]{1,0:T(8,128)(2,1)S(1)}, u32[]{:S(2)}, u32[]{:S(2)}) %collective-permute-start.5) | collective-permute-done | bytes 491552 | tf_op jit(solution)/shard_map/ppermute | solution.py:14
  174.5 0.1 constant_dynamic-update-slice_fusion.9
  174.5 10.4 %collective-permute-done.6 = bf16[384,640]{1,0:T(8,128)(2,1)S(1)} collective-permute-done((bf16[384,640]{1,0:T(8,128)(2,1)S(1)}, bf16[384,640]{1,0:T(8,128)(2,1)S(1)}, u32[]{:S(2)}, u32[]{:S(2)}) %collective-permute-start.6) | collective-permute-done | bytes 491552 | tf_op jit(solution)/shard_map/ppermute | solution.py:14
  184.9 0.1 constant_dynamic-update-slice_fusion.8
  185.0 10.5 %collective-permute-done.7 = bf16[384,640]{1,0:T(8,128)(2,1)S(1)} collective-permute-done((bf16[384,640]{1,0:T(8,128)(2,1)S(1)}, bf16[384,640]{1,0:T(8,128)(2,1)S(1)}, u32[]{:S(2)}, u32[]{:S(2)}) %collective-permute-start.7) | collective-permute-done | bytes 491552 | tf_op jit(solution)/shard_map/ppermute | solution.py:14
  195.4 0.1 constant_dynamic-update-slice_fusion.7
  195.5 0.1 constant_dynamic-update-slice_fusion
  195.6 0.1 constant_dynamic-update-slice_fusion.6
  195.7 0.9 fusion.96
  196.6 0.6 fusion.5
  197.3 0.9 fusion.97
  198.1 0.6 fusion.7
  198.8 0.9 fusion.98
  199.7 0.6 fusion.9
  200.3 0.9 fusion.99
  201.2 0.6 fusion.11
  201.8 0.9 fusion.100
  202.7 0.6 fusion.13
  203.4 0.7 fusion.72
  204.1 0.7 fusion.66
  204.8 0.8 fusion.60
  205.6 0.7 fusion.54
  206.4 0.7 fusion.48
  207.1 0.0 all-gather.2.cloned.1.call-done
  207.1 8.9 %convolution_convert_fusion = bf16[384,5120]{1,0:T(8,128)(2,1)} fusion(bf16[384,640]{1,0:T(8,128)(2,1)S(1)} %fusion.48, bf16[640,5120]{0,1:T(8,128)(2,1)} %all-gather.2.cloned.1.call-done), kind=kOutput, calls=%fused_computation | convolution fusion | flops 2518548480 | bytes 10977280 | tf_op jit(solution)/shard_map/dot_general | solution.py:67
  216.1 6.3 %copy.9 = bf16[384,5120]{0,1:T(8,128)(2,1)} copy(bf16[384,5120]{1,0:T(8,128)(2,1)} %convolution_convert_fusion) | data formatting | bytes 7864320
  222.3 0.0 reduce-scatter.4.cloned.1.call-update
  222.4 69.3 %reduce-scatter.4.cloned.1.call-done = bf16[640,384]{1,0:T(8,128)(2,1)} async-done(((bf16[5120,384]{1,0:T(8,128)(2,1)}), bf16[640,384]{1,0:T(8,128)(2,1)}) %reduce-scatter.4.cloned.1.call-update) | async-done | bytes 491536
  291.6 2.0 copy.10
  (9 shorter events, 0.0 us)
Async XLA Ops:
  6.5 157.3 %copy-start = (bf16[384,640]{1,0:T(8,128)(2,1)S(1)}, bf16[384,640]{1,0:T(8,128)(2,1)}, u32[]{:S(2)}) copy-start(bf16[384,640]{1,0:T(8,128)(2,1)} %param.10) | copy-start | bytes 1474564
  6.5 200.6 %all-gather.2.cloned.1.call-start = ((), (), s32[]{:S(2)}) async-start(), calls=%async_computation.1 | async-start | bytes 6656000 | tf_op jit(solution)/shard_map/all_gather | solution.py:69
  7.3 284.4 %reduce-scatter.4.cloned.1.call-start = ((), (), s32[]{:S(2)}) async-start(), calls=%async_computation.2 | async-start | bytes 4423680
  7.3 154.1 %collective-permute-start = (bf16[384,640]{1,0:T(8,128)(2,1)}, bf16[384,640]{1,0:T(8,128)(2,1)S(1)}, u32[]{:S(2)}, u32[]{:S(2)}) collective-permute-start(bf16[384,640]{1,0:T(8,128)(2,1)} %param.9), channel_id=1, source_target_pairs={{0,8},{8,16},{16,24},{24,32},{32,40},{40,48},{48,56},{56,64},{64,7... | collective-permute-start | bytes 1474568 | tf_op jit(solution)/shard_map/ppermute | solution.py:14
  11.8 152.0 %collective-permute-start.1 = (bf16[384,640]{1,0:T(8,128)(2,1)}, bf16[384,640]{1,0:T(8,128)(2,1)S(1)}, u32[]{:S(2)}, u32[]{:S(2)}) collective-permute-start(bf16[384,640]{1,0:T(8,128)(2,1)} %param.9), channel_id=1, source_target_pairs={{0,16},{8,24},{16,32},{24,40},{32,48},{40,56},{48,64},{56,72},{64,... | collective-permute-start | bytes 1474568 | tf_op jit(solution)/shard_map/ppermute | solution.py:14
  15.0 153.6 %collective-permute-start.2 = (bf16[384,640]{1,0:T(8,128)(2,1)}, bf16[384,640]{1,0:T(8,128)(2,1)S(1)}, u32[]{:S(2)}, u32[]{:S(2)}) collective-permute-start(bf16[384,640]{1,0:T(8,128)(2,1)} %param.9), channel_id=1, source_target_pairs={{0,24},{8,32},{16,40},{24,48},{32,56},{40,64},{48,72},{56,80},{64,... | collective-permute-start | bytes 1474568 | tf_op jit(solution)/shard_map/ppermute | solution.py:14
  18.4 152.5 %collective-permute-start.3 = (bf16[384,640]{1,0:T(8,128)(2,1)}, bf16[384,640]{1,0:T(8,128)(2,1)S(1)}, u32[]{:S(2)}, u32[]{:S(2)}) collective-permute-start(bf16[384,640]{1,0:T(8,128)(2,1)} %param.9), channel_id=1, source_target_pairs={{0,32},{8,40},{16,48},{24,56},{32,64},{40,72},{48,80},{56,88},{64,... | collective-permute-start | bytes 1474568 | tf_op jit(solution)/shard_map/ppermute | solution.py:14
  21.9 149.1 %collective-permute-start.4 = (bf16[384,640]{1,0:T(8,128)(2,1)}, bf16[384,640]{1,0:T(8,128)(2,1)S(1)}, u32[]{:S(2)}, u32[]{:S(2)}) collective-permute-start(bf16[384,640]{1,0:T(8,128)(2,1)} %param.10), channel_id=1, source_target_pairs={{0,8},{8,16},{16,24},{24,32},{32,40},{40,48},{48,56},{56,64},{64,7... | collective-permute-start | bytes 1474568 | tf_op jit(solution)/shard_map/ppermute | solution.py:14
  161.4 13.1 %collective-permute-start.5 = (bf16[384,640]{1,0:T(8,128)(2,1)}, bf16[384,640]{1,0:T(8,128)(2,1)S(1)}, u32[]{:S(2)}, u32[]{:S(2)}) collective-permute-start(bf16[384,640]{1,0:T(8,128)(2,1)} %param.10), channel_id=1, source_target_pairs={{0,16},{8,24},{16,32},{24,40},{32,48},{40,56},{48,64},{56,72},{64,... | collective-permute-start | bytes 1474568 | tf_op jit(solution)/shard_map/ppermute | solution.py:14
  163.8 21.1 %collective-permute-start.6 = (bf16[384,640]{1,0:T(8,128)(2,1)S(1)}, bf16[384,640]{1,0:T(8,128)(2,1)S(1)}, u32[]{:S(2)}, u32[]{:S(2)}) collective-permute-start(bf16[384,640]{1,0:T(8,128)(2,1)S(1)} %copy-done), channel_id=1, source_target_pairs={{0,24},{8,32},{16,40},{24,48},{32,56},{40,64},{48,72},{56,80},{64,... | collective-permute-start | bytes 1474568 | tf_op jit(solution)/shard_map/ppermute | solution.py:14
  168.6 26.9 %collective-permute-start.7 = (bf16[384,640]{1,0:T(8,128)(2,1)S(1)}, bf16[384,640]{1,0:T(8,128)(2,1)S(1)}, u32[]{:S(2)}, u32[]{:S(2)}) collective-permute-start(bf16[384,640]{1,0:T(8,128)(2,1)S(1)} %copy-done), channel_id=1, source_target_pairs={{0,32},{8,40},{16,48},{24,56},{32,64},{40,72},{48,80},{56,88},{64,... | collective-permute-start | bytes 1474568 | tf_op jit(solution)/shard_map/ppermute | solution.py:14
  170.9 24.8 %copy-start.1 = (bf16[384,640]{1,0:T(8,128)(2,1)S(1)}, bf16[384,640]{1,0:T(8,128)(2,1)}, u32[]{:S(2)}) copy-start(bf16[384,640]{1,0:T(8,128)(2,1)} %param.8) | copy-start | bytes 1474564
Sparse Core Ops, SparseCore 0:
  10.6 113.0 all-gather.1
  222.5 69.0 reduce-scatter.3
where the time goes:
time: 301 us; the launch traced here: 300 us
  blocking collectives  123 us (41%)
  waiting for transfers between devices  94.2 us (31%)
  starting transfers between devices  27.5 us (9%)
  matrix products  17.1 us (6%)
  between operations  17 us (6%)
  local copies, waits for them, and re-layouts  15.4 us (5%)
  other arithmetic  6.31 us (2%)
    all_gather x1, blocking collectives, on_device(): lax.all_gather(text_keys, 'tm', axis=0, tiled=True)  74.3 us
    unnamed x3, waiting for transfers between devices  70 us
    all_gather x1, blocking collectives, on_device(): lax.all_gather(text_values, 'tm', axis=0, tiled=True)  48.6 us
    ppermute x8, starting transfers between devices, from_behind(): lax.ppermute(value, axis, [(source, source + steps) for source in range(i...  27.5 us
    ppermute x8, waiting for transfers between devices, from_behind(): lax.ppermute(value, axis, [(source, source + steps) for source in range(i...  24.2 us
    unnamed x21, local copies, waits for them, and re-layouts  12.2 us
    dot_general x1, matrix products, on_device(): jnp.dot(attended_all, lax.all_gather(out_weight, 'tm', axis=1, tiled=True...  8.94 us
  transfers between devices with their start and end apart: 10, of which 4 were waited for; matrix products, arithmetic and copies ran while one was open for 7% of the time, Pallas kernels for 0%

commit v1 on v0

--- a/solution.py
+++ b/solution.py
@@ -20,8 +20,15 @@
     local_heads = width // HD
     scale = 1.0 / math.sqrt(HD)
     position = lax.axis_index("tm")
+
+    def feed_the_strips_all(a0):
+        carry = lax.all_to_all(
+            jnp.stack(lax.axis_size("tm") * [a0], 0), axis_name="tm", split_axis=0, concat_axis=0
+        )
+        return jnp.concatenate(carry, 0)
+
     text_k, text_v = (
-        lax.all_gather(text_keys, "tm", axis=0, tiled=True),
+        feed_the_strips_all(text_keys),
         lax.all_gather(text_values, "tm", axis=0, tiled=True),
     )
     key_list = [keys]

time: 301 us -> 289 us (0.960)
  blocking collectives: 123 us -> 90.8 us
  local copies, waits for them, and re-layouts: 15.4 us -> 27.9 us
  starting transfers between devices: 27.5 us -> 36.8 us
  waiting for transfers between devices: 94.2 us -> 85.2 us
  matrix products: 17.1 us -> 23.5 us
    all_gather x1 -> x0, blocking collectives: 74.3 us -> none  [on_device(): lax.all_gather(text_keys, 'tm', axis=0, tiled=True)]
    all_gather x1, blocking collectives: 48.6 us -> 90.8 us  [on_device(): lax.all_gather(text_values, 'tm', axis=0, tiled=True)]
    unnamed x21, local copies, waits for them, and re-layouts: 12.2 us -> 21.1 us
    all_to_all x0 -> x1, starting transfers between devices: none -> 8.38 us  [feed_the_strips_all(): lax.all_to_all(jnp.stack(lax.axis_size('tm') * [a0], 0), axis_name='tm',...]
    ppermute x8, waiting for transfers between devices: 24.2 us -> 16.2 us  [from_behind(): lax.ppermute(value, axis, [(source, source + steps) for source in range(i...]
    dot_general x5, matrix products: 3.71 us -> 9.22 us  [on_device(): jnp.dot(weights.astype(jnp.bfloat16), value_h, preferred_element_type=jnp...]
  transfers between devices with their start and end apart: 10 -> 11, of which waited for: 4 -> 3; matrix products, arithmetic and copies ran while one was open for 7% -> 14% of each run, Pallas kernels for 0% -> 0%
where the time goes in v1:
time: 289 us; the launch traced here: 287 us
  blocking collectives  90.8 us (31%)
  waiting for transfers between devices  85.2 us (29%)
  starting transfers between devices  36.8 us (13%)
  local copies, waits for them, and re-layouts  27.9 us (10%)
  matrix products  23.5 us (8%)
  between operations  16.8 us (6%)
  other arithmetic  6.31 us (2%)
    all_gather x1, blocking collectives, on_device(): lax.all_gather(text_values, 'tm', axis=0, tiled=True)  90.8 us
    unnamed x3, waiting for transfers between devices  69 us
    ppermute x8, starting transfers between devices, from_behind(): lax.ppermute(value, axis, [(source, source + steps) for source in range(i...  28.4 us
    unnamed x21, local copies, waits for them, and re-layouts  21.1 us
    ppermute x8, waiting for transfers between devices, from_behind(): lax.ppermute(value, axis, [(source, source + steps) for source in range(i...  16.2 us
    dot_general x5, matrix products, on_device(): jnp.dot(weights.astype(jnp.bfloat16), value_h, preferred_element_type=jnp...  9.22 us
    dot_general x1, matrix products, on_device(): jnp.dot(attended_all, lax.all_gather(out_weight, 'tm', axis=1, tiled=True...  8.93 us
    all_to_all x1, starting transfers between devices, feed_the_strips_all(): lax.all_to_all(jnp.stack(lax.axis_size('tm') * [a0], 0), axis_name='tm',...  8.38 us
  transfers between devices with their start and end apart: 11, of which 3 were waited for; matrix products, arithmetic and copies ran while one was open for 14% of the time, Pallas kernels for 0%

profile of v1, /device:TPU:1, one launch (start us, length us, event | category | flops | bytes accessed | tf_op | source)
XLA Modules:
  0.0 287.2 jit_solution(8477077985667173023)
XLA Ops:
  6.5 0.7 all-gather.2.cloned.1.call-update
  7.3 4.5 %collective-permute-start = (bf16[384,640]{1,0:T(8,128)(2,1)}, bf16[384,640]{1,0:T(8,128)(2,1)}, u32[]{:S(2)}, u32[]{:S(2)}) collective-permute-start(bf16[384,640]{1,0:T(8,128)(2,1)} %param.9), channel_id=1, source_target_pairs={{0,8},{8,16},{16,24},{24,32},{32,40},{40,48},{48,56},{56,64},{64,7... | collective-permute-start | bytes 1474568 | tf_op jit(solution)/shard_map/ppermute | solution.py:14
  11.8 3.9 %collective-permute-start.1 = (bf16[384,640]{1,0:T(8,128)(2,1)}, bf16[384,640]{1,0:T(8,128)(2,1)}, u32[]{:S(2)}, u32[]{:S(2)}) collective-permute-start(bf16[384,640]{1,0:T(8,128)(2,1)} %param.9), channel_id=1, source_target_pairs={{0,16},{8,24},{16,32},{24,40},{32,48},{40,56},{48,64},{56,72},{64,... | collective-permute-start | bytes 1474568 | tf_op jit(solution)/shard_map/ppermute | solution.py:14
  15.7 3.5 %collective-permute-start.2 = (bf16[384,640]{1,0:T(8,128)(2,1)}, bf16[384,640]{1,0:T(8,128)(2,1)}, u32[]{:S(2)}, u32[]{:S(2)}) collective-permute-start(bf16[384,640]{1,0:T(8,128)(2,1)} %param.9), channel_id=1, source_target_pairs={{0,24},{8,32},{16,40},{24,48},{32,56},{40,64},{48,72},{56,80},{64,... | collective-permute-start | bytes 1474568 | tf_op jit(solution)/shard_map/ppermute | solution.py:14
  19.2 3.5 %collective-permute-start.3 = (bf16[384,640]{1,0:T(8,128)(2,1)}, bf16[384,640]{1,0:T(8,128)(2,1)}, u32[]{:S(2)}, u32[]{:S(2)}) collective-permute-start(bf16[384,640]{1,0:T(8,128)(2,1)} %param.9), channel_id=1, source_target_pairs={{0,32},{8,40},{16,48},{24,56},{32,64},{40,72},{48,80},{56,88},{64,... | collective-permute-start | bytes 1474568 | tf_op jit(solution)/shard_map/ppermute | solution.py:14
  22.6 1.6 stack.2
  24.3 8.4 %all-to-all-start = ((bf16[64,8,640]{2,1,0:T(8,128)(2,1)}), bf16[64,8,640]{2,1,0:T(8,128)(2,1)}, u32[]{:S(2)}, u32[]{:S(2)}) async-start(bf16[64,8,640]{2,1,0:T(8,128)(2,1)} %stack.2), calls=%async_computation | async-start | bytes 1310720 | tf_op jit(solution)/shard_map/all_to_all | solution.py:25
  32.6 0.0 reduce-scatter.4.cloned.1.call-start
  32.7 3.5 %collective-permute-start.4 = (bf16[384,640]{1,0:T(8,128)(2,1)}, bf16[384,640]{1,0:T(8,128)(2,1)}, u32[]{:S(2)}, u32[]{:S(2)}) collective-permute-start(bf16[384,640]{1,0:T(8,128)(2,1)} %param.10), channel_id=1, source_target_pairs={{0,8},{8,16},{16,24},{24,32},{32,40},{40,48},{48,56},{56,64},{64,7... | collective-permute-start | bytes 1474568 | tf_op jit(solution)/shard_map/ppermute | solution.py:14
  36.3 1.3 dynamic_slice.18
  38.8 1.5 fusion.95
  40.3 0.6 fusion.90
  41.0 1.1 constant_dynamic-update-slice_fusion.4
  42.1 90.8 %all_gather.6 = bf16[512,640]{1,0:T(8,128)(2,1)} all-gather(bf16[8,640]{1,0:T(8,128)(2,1)} %param.12), channel_id=1, replica_groups=mesh['tm'=64,'head'=8] {'tm'}, dimensions={0}, use_global_device_ids=true | all-gather | bytes 665600 | tf_op jit(solution)/shard_map/all_gather | solution.py:32
  132.8 0.6 fusion.91
  134.1 0.6 fusion.92
  135.3 0.6 fusion.93
  136.6 0.7 fusion.94
  137.3 0.3 dynamic-update-slice.17
  137.5 0.2 dynamic-update-slice.18
  137.7 0.2 dynamic-update-slice.19
  137.9 0.2 dynamic-update-slice.20
  138.1 0.2 dynamic-update-slice.21
  138.4 0.2 dynamic-update-slice.22
  138.6 1.9 constant_dynamic-update-slice_fusion.10
  140.5 1.4 collective-permute-start.5
  141.9 1.1 constant_dynamic-update-slice_fusion.3
  143.0 4.8 %collective-permute-start.6 = (bf16[384,640]{1,0:T(8,128)(2,1)}, bf16[384,640]{1,0:T(8,128)(2,1)S(1)}, u32[]{:S(2)}, u32[]{:S(2)}) collective-permute-start(bf16[384,640]{1,0:T(8,128)(2,1)} %param.10), channel_id=1, source_target_pairs={{0,24},{8,32},{16,40},{24,48},{32,56},{40,64},{48,72},{56,80},{64,... | collective-permute-start | bytes 1474568 | tf_op jit(solution)/shard_map/ppermute | solution.py:14
  147.8 1.1 constant_dynamic-update-slice_fusion.2
  148.9 0.0 collective-permute-done.2
  148.9 3.2 %collective-permute-start.7 = (bf16[384,640]{1,0:T(8,128)(2,1)}, bf16[384,640]{1,0:T(8,128)(2,1)S(1)}, u32[]{:S(2)}, u32[]{:S(2)}) collective-permute-start(bf16[384,640]{1,0:T(8,128)(2,1)} %param.10), channel_id=1, source_target_pairs={{0,32},{8,40},{16,48},{24,56},{32,64},{40,72},{48,80},{56,88},{64,... | collective-permute-start | bytes 1474568 | tf_op jit(solution)/shard_map/ppermute | solution.py:14
  152.1 1.1 constant_dynamic-update-slice_fusion.1
  153.2 0.0 collective-permute-done.3
  153.2 1.1 constant_dynamic-update-slice_fusion
  154.3 1.9 constant_dynamic-update-slice_fusion.9
  156.2 0.8 constant_dynamic-update-slice_fusion.8
  157.0 6.5 %collective-permute-done.6 = bf16[384,640]{1,0:T(8,128)(2,1)S(1)} collective-permute-done((bf16[384,640]{1,0:T(8,128)(2,1)}, bf16[384,640]{1,0:T(8,128)(2,1)S(1)}, u32[]{:S(2)}, u32[]{:S(2)}) %collective-permute-start.6) | collective-permute-done | bytes 491552 | tf_op jit(solution)/shard_map/ppermute | solution.py:14
  163.5 0.9 constant_dynamic-update-slice_fusion.7
  164.4 9.7 %collective-permute-done.7 = bf16[384,640]{1,0:T(8,128)(2,1)S(1)} collective-permute-done((bf16[384,640]{1,0:T(8,128)(2,1)}, bf16[384,640]{1,0:T(8,128)(2,1)S(1)}, u32[]{:S(2)}, u32[]{:S(2)}) %collective-permute-start.7) | collective-permute-done | bytes 491552 | tf_op jit(solution)/shard_map/ppermute | solution.py:14
  174.0 0.9 constant_dynamic-update-slice_fusion.6
  174.9 1.0 constant_dynamic-update-slice_fusion.5
  175.9 1.2 bitcast_dynamic-update-slice_fusion
  177.0 0.0 copy-start.1
  177.1 1.8 fusion.96
  178.9 0.6 fusion.5
  179.5 0.9 fusion.97
  180.4 0.6 fusion.7
  181.0 0.9 fusion.98
  181.9 0.6 fusion.9
  182.5 0.9 fusion.99
  183.4 0.6 fusion.11
  184.0 0.9 fusion.100
  184.9 0.6 fusion.13
  185.5 1.9 fusion.72
  187.4 1.8 fusion.66
  189.2 1.8 fusion.60
  191.1 1.8 fusion.54
  192.9 1.8 fusion.48
  194.8 0.0 all-gather.2.cloned.1.call-done
  194.8 8.9 %convolution_convert_fusion = bf16[384,5120]{1,0:T(8,128)(2,1)} fusion(bf16[384,640]{1,0:T(8,128)(2,1)S(1)} %fusion.48, bf16[640,5120]{0,1:T(8,128)(2,1)} %all-gather.2.cloned.1.call-done), kind=kOutput, calls=%fused_computation | convolution fusion | flops 2518548480 | bytes 10977280 | tf_op jit(solution)/shard_map/dot_general | solution.py:74
  203.8 6.3 %copy.9 = bf16[384,5120]{0,1:T(8,128)(2,1)} copy(bf16[384,5120]{1,0:T(8,128)(2,1)} %convolution_convert_fusion) | data formatting | bytes 7864320
  210.0 0.0 reduce-scatter.4.cloned.1.call-update
  210.0 68.3 %reduce-scatter.4.cloned.1.call-done = bf16[640,384]{1,0:T(8,128)(2,1)} async-done(((bf16[5120,384]{1,0:T(8,128)(2,1)}), bf16[640,384]{1,0:T(8,128)(2,1)}) %reduce-scatter.4.cloned.1.call-update) | async-done | bytes 491536
  278.4 2.0 copy.10
  (11 shorter events, 0.0 us)
Async XLA Ops:
  6.5 188.3 %all-gather.2.cloned.1.call-start = ((), (), s32[]{:S(2)}) async-start(), calls=%async_computation.2 | async-start | bytes 6656000 | tf_op jit(solution)/shard_map/all_gather | solution.py:76
  7.3 133.2 %collective-permute-start = (bf16[384,640]{1,0:T(8,128)(2,1)}, bf16[384,640]{1,0:T(8,128)(2,1)}, u32[]{:S(2)}, u32[]{:S(2)}) collective-permute-start(bf16[384,640]{1,0:T(8,128)(2,1)} %param.9), channel_id=1, source_target_pairs={{0,8},{8,16},{16,24},{24,32},{32,40},{40,48},{48,56},{56,64},{64,7... | collective-permute-start | bytes 1474568 | tf_op jit(solution)/shard_map/ppermute | solution.py:14
  11.8 131.2 %collective-permute-start.1 = (bf16[384,640]{1,0:T(8,128)(2,1)}, bf16[384,640]{1,0:T(8,128)(2,1)}, u32[]{:S(2)}, u32[]{:S(2)}) collective-permute-start(bf16[384,640]{1,0:T(8,128)(2,1)} %param.9), channel_id=1, source_target_pairs={{0,16},{8,24},{16,32},{24,40},{32,48},{40,56},{48,64},{56,72},{64,... | collective-permute-start | bytes 1474568 | tf_op jit(solution)/shard_map/ppermute | solution.py:14
  15.7 133.2 %collective-permute-start.2 = (bf16[384,640]{1,0:T(8,128)(2,1)}, bf16[384,640]{1,0:T(8,128)(2,1)}, u32[]{:S(2)}, u32[]{:S(2)}) collective-permute-start(bf16[384,640]{1,0:T(8,128)(2,1)} %param.9), channel_id=1, source_target_pairs={{0,24},{8,32},{16,40},{24,48},{32,56},{40,64},{48,72},{56,80},{64,... | collective-permute-start | bytes 1474568 | tf_op jit(solution)/shard_map/ppermute | solution.py:14
  19.2 134.1 %collective-permute-start.3 = (bf16[384,640]{1,0:T(8,128)(2,1)}, bf16[384,640]{1,0:T(8,128)(2,1)}, u32[]{:S(2)}, u32[]{:S(2)}) collective-permute-start(bf16[384,640]{1,0:T(8,128)(2,1)} %param.9), channel_id=1, source_target_pairs={{0,32},{8,40},{16,48},{24,56},{32,64},{40,72},{48,80},{56,88},{64,... | collective-permute-start | bytes 1474568 | tf_op jit(solution)/shard_map/ppermute | solution.py:14
  24.3 151.6 %all-to-all-start = ((bf16[64,8,640]{2,1,0:T(8,128)(2,1)}), bf16[64,8,640]{2,1,0:T(8,128)(2,1)}, u32[]{:S(2)}, u32[]{:S(2)}) async-start(bf16[64,8,640]{2,1,0:T(8,128)(2,1)} %stack.2), calls=%async_computation | async-start | bytes 1310720 | tf_op jit(solution)/shard_map/all_to_all | solution.py:25
  32.6 245.7 %reduce-scatter.4.cloned.1.call-start = ((), (), s32[]{:S(2)}) async-start(), calls=%async_computation.3 | async-start | bytes 4423680
  32.7 121.6 %collective-permute-start.4 = (bf16[384,640]{1,0:T(8,128)(2,1)}, bf16[384,640]{1,0:T(8,128)(2,1)}, u32[]{:S(2)}, u32[]{:S(2)}) collective-permute-start(bf16[384,640]{1,0:T(8,128)(2,1)} %param.10), channel_id=1, source_target_pairs={{0,8},{8,16},{16,24},{24,32},{32,40},{40,48},{48,56},{56,64},{64,7... | collective-permute-start | bytes 1474568 | tf_op jit(solution)/shard_map/ppermute | solution.py:14
  140.5 34.4 %copy-start = (bf16[512,640]{1,0:T(8,128)(2,1)S(1)}, bf16[512,640]{1,0:T(8,128)(2,1)}, u32[]{:S(2)}) copy-start(bf16[512,640]{1,0:T(8,128)(2,1)} %all_gather.6) | copy-start | bytes 1966084
  140.5 15.7 %collective-permute-start.5 = (bf16[384,640]{1,0:T(8,128)(2,1)}, bf16[384,640]{1,0:T(8,128)(2,1)S(1)}, u32[]{:S(2)}, u32[]{:S(2)}) collective-permute-start(bf16[384,640]{1,0:T(8,128)(2,1)} %param.10), channel_id=1, source_target_pairs={{0,16},{8,24},{16,32},{24,40},{32,48},{40,56},{48,64},{56,72},{64,... | collective-permute-start | bytes 1474568 | tf_op jit(solution)/shard_map/ppermute | solution.py:14
  143.0 20.5 %collective-permute-start.6 = (bf16[384,640]{1,0:T(8,128)(2,1)}, bf16[384,640]{1,0:T(8,128)(2,1)S(1)}, u32[]{:S(2)}, u32[]{:S(2)}) collective-permute-start(bf16[384,640]{1,0:T(8,128)(2,1)} %param.10), channel_id=1, source_target_pairs={{0,24},{8,32},{16,40},{24,48},{32,56},{40,64},{48,72},{56,80},{64,... | collective-permute-start | bytes 1474568 | tf_op jit(solution)/shard_map/ppermute | solution.py:14
  148.9 25.1 %collective-permute-start.7 = (bf16[384,640]{1,0:T(8,128)(2,1)}, bf16[384,640]{1,0:T(8,128)(2,1)S(1)}, u32[]{:S(2)}, u32[]{:S(2)}) collective-permute-start(bf16[384,640]{1,0:T(8,128)(2,1)} %param.10), channel_id=1, source_target_pairs={{0,32},{8,40},{16,48},{24,56},{32,64},{40,72},{48,80},{56,88},{64,... | collective-permute-start | bytes 1474568 | tf_op jit(solution)/shard_map/ppermute | solution.py:14
  177.0 2.5 copy-start.1
Sparse Core Ops, SparseCore 0:
  10.6 115.6 all-gather.1
  210.2 68.1 reduce-scatter.3
